TPU v7x, 256 devices: a whole 4x4x8 slice. The times are simulated.
256 devices in a mesh: link: 64 (over x, z, core), col: 4 (over y).
Axes of the slice: x: 4, y: 4, z: 8, core: 2. Of those that a mesh axis runs over, the one named last changes fastest.
Arguments:
- values: bfloat16 [1024, 16, 128], P('link'), may hold values from -6 to 6
- tiles: int32 [1024, 16], P('link'), may hold values from 0 to 127, all different within a row
- barrier: float32 [1024], P('link'), may hold values from 0.5 to 2
- slack: float32 [16384], replicated, may hold values from 0.5 to 2
- order: int32 [128], replicated, may hold values from 0 to 127, each once
Outputs:
- factored: float32 [16384, 16384], P('link', 'col')
Inputs may be any that keep to these rules, and one draw needn't show every extreme that they name: `tiles`: each commodity's 16 tile numbers are distinct, and every tile is named by some commodity. `order`: each tile number appears once.
All inputs are finite; a program needn't handle non-finite values.
Results may differ from a plain program's by a relative error of at most 0.0038.
Values may be sent and summed in bfloat16 or wider, within the bound.
No kernel may reach another device: no remote copies, remote signals or barrier semaphores. Data moves between devices by JAX's collectives and lax.ppermute only.
A program may use at most 64 MiB of HBM per device.

v0:
```python
import jax
import jax.numpy as jnp
from jax import lax
from jax.sharding import PartitionSpec as P

PANEL = 128


def spread(value, axis, source):
    kept = jnp.where(lax.axis_index(axis) == source, value, 0).astype(value.dtype)
    return lax.psum(kept, axis)


def densify(tile_vals, tile_ids, targets):
    onehot = (tile_ids[:, :, None] == targets[None, None, :]).astype(jnp.bfloat16)
    dense_out = jnp.einsum("kjp,kju->kpu", onehot, tile_vals, preferred_element_type=jnp.float32)
    dense_out = dense_out.astype(jnp.bfloat16)
    return dense_out.reshape(tile_vals.shape[0], targets.shape[0] * tile_vals.shape[2])


def contract_rows(left_side, right_side):
    return lax.dot_general(
        left_side, right_side, (((0,), (0,)), ((), ())), preferred_element_type=jnp.float32
    )


def local(values, tiles, barrier, slack, order):
    link_devs = lax.axis_size("link")
    col_devs = lax.axis_size("col")
    link_idx = lax.axis_index("link")
    col_idx = lax.axis_index("col")
    link_count = slack.shape[0]
    rows_dev = link_count // link_devs
    cols_dev = link_count // col_devs
    tile_len = values.shape[2]
    ntiles = order.shape[0]
    factor = link_count / (values.shape[0] * link_devs * values.shape[1] * tile_len)
    scaled = (jnp.sqrt(barrier * factor)[:, None, None] * values.astype(jnp.float32)).astype(
        jnp.bfloat16
    )
    own_dense = densify(scaled, tiles, order)
    link_rows = lax.all_to_all(own_dense, "link", split_axis=1, concat_axis=0, tiled=True)
    col_slab = lax.dynamic_slice_in_dim(own_dense, col_idx * cols_dev, cols_dev, 1)
    normal = contract_rows(link_rows, lax.all_gather(col_slab, "link", axis=0, tiled=True))
    rows_g = link_idx * rows_dev + jnp.arange(rows_dev)
    cols_g = col_idx * cols_dev + jnp.arange(cols_dev)
    perm_hot = (order[:, None] == jnp.arange(ntiles)[None, :]).astype(jnp.float32)
    slack_ord = jnp.dot(
        perm_hot, slack.reshape(ntiles, tile_len), precision=lax.Precision.HIGHEST
    ).reshape(link_count)
    slack_rows = lax.dynamic_slice_in_dim(slack_ord, link_idx * rows_dev, rows_dev)
    matrix = normal + jnp.where(
        rows_g[:, None] == cols_g[None, :], slack_rows[:, None], jnp.float32(0.0)
    )
    panels = []
    for panel_no in range(2):
        first_col = panel_no * PANEL
        diag_block = matrix[first_col : first_col + PANEL, first_col : first_col + PANEL]
        factor_local = jnp.linalg.cholesky(diag_block)
        lower_fac = spread(factor_local, "link", 0)
        solved = jax.scipy.linalg.solve_triangular(
            lower_fac, matrix[:, first_col : first_col + PANEL].T, lower=True
        ).T
        picker = ((rows_g - first_col)[:, None] == jnp.arange(PANEL)[None, :]).astype(jnp.float32)
        diag_rows = jnp.dot(picker, lower_fac, precision=lax.Precision.HIGHEST)
        column = jnp.where(
            rows_g[:, None] < first_col,
            jnp.float32(0.0),
            jnp.where(rows_g[:, None] < first_col + PANEL, diag_rows, solved),
        )
        across = spread(column.astype(jnp.bfloat16), "col", 0)
        everyone = lax.all_gather(across, "link", axis=0, tiled=True)
        col_part = lax.dynamic_slice_in_dim(everyone, col_idx * cols_dev, cols_dev, 0)
        matrix = matrix - lax.dot_general(
            across, col_part, (((1,), (1,)), ((), ())), preferred_element_type=jnp.float32
        )
        panels.append(column)
    panel_block = jnp.concatenate(panels, 1)
    padded = jnp.pad(panel_block, ((0, 0), (0, cols_dev - 2 * PANEL)))
    return jnp.where(
        cols_g[None, :] < 2 * PANEL,
        padded,
        jnp.where(rows_g[:, None] < 2 * PANEL, jnp.float32(0.0), matrix),
    )


def solution(mesh):
    in_specs = (P("link", None, None), P("link", None), P("link"), P(), P())
    out_specs = P("link", "col")
    return jax.shard_map(local, mesh=mesh, in_specs=in_specs, out_specs=out_specs, check_vma=False)
```

profile of v0, /device:TPU:1, one launch (start us, length us, event | category | flops | bytes accessed | tf_op | source)
XLA Modules:
  0.0 768.8 jit_solution(11925922518593524493)
XLA Ops:
  7.2 1.4 convolution_convert_fusion
  10.9 13.0 %all-to-all-start = ((bf16[16,64,256]{2,0,1:T(8,128)(2,1)}), bf16[16,64,256]{2,0,1:T(8,128)(2,1)S(1)}, u32[]{:S(2)}, u32[]{:S(2)}) async-start(bf16[16,64,256]{2,0,1:T(8,128)(2,1)} %copy.12), calls=%async_computation | async-start | bytes 1048576 | tf_op jit(solution)/shard_map/all_to_all | solution.py:42
  24.3 19.3 %all-to-all-done = bf16[16,64,256]{2,0,1:T(8,128)(2,1)S(1)} async-done(((bf16[16,64,256]{2,0,1:T(8,128)(2,1)}), bf16[16,64,256]{2,0,1:T(8,128)(2,1)S(1)}, u32[]{:S(2)}, u32[]{:S(2)}) %all-to-all-start) | async-done | bytes 524320 | tf_op jit(solution)/shard_map/all_to_all | solution.py:42
  43.6 54.6 %all-gather.4.cloned.1.call-done = bf16[1024,4096]{1,0:T(8,128)(2,1)} async-done(((bf16[16,4096]{1,0:T(8,128)(2,1)}), bf16[1024,4096]{1,0:T(8,128)(2,1)}) %all-gather.4.cloned.1.call-update) | async-done | bytes 8388624 | tf_op jit(solution)/shard_map/all_gather | solution.py:44
  98.2 6.6 convolution_add_fusion
  104.8 2.0 copy-done.1
  107.8 11.7 %cholesky.44 = f32[128,128]{1,0:T(8,128)S(1)} custom-call(f32[128,128]{1,0:T(8,128)S(1)} %fusion.14), custom_call_target="Cholesky" | custom-call | tf_op jit(solution)/shard_map/jit(cholesky)/cholesky | solution.py:59
  120.2 1.3 select_select_fusion.1
  121.6 167.5 %all-reduce.6.cloned.1.call-done = f32[128,128]{1,0:T(8,128)} async-done(((f32[128,128]{1,0:T(8,128)}), f32[128,128]{1,0:T(8,128)}) %all-reduce.6.cloned.1.call-update) | async-done | bytes 65552 | tf_op jit(solution)/shard_map/psum | solution.py:11
  289.9 9.8 %custom-call.6 = f32[1,128,128]{1,2,0:T(8,128)S(1)} custom-call(f32[1,128,128]{2,1,0:T(8,128)S(1)} %select_bitcast_fusion.1), custom_call_target="InvertDiagBlocksLowerTriangular" | custom-call | tf_op jit(solution)/shard_map/jit(_solve_triangular)/triangular_solve | solution.py:61
  300.9 1.9 convert_select_fusion.1
  302.8 41.2 %all-reduce.8.cloned.1.call-done = bf16[256,128]{0,1:T(8,128)(2,1)} async-done(((bf16[256,128]{0,1:T(8,128)(2,1)}), bf16[256,128]{0,1:T(8,128)(2,1)}) %all-reduce.8.cloned.1.call-update) | async-done | bytes 65552 | tf_op jit(solution)/shard_map/psum | solution.py:11
  344.3 81.0 %all-gather.6.cloned.1.call-done = bf16[16384,128]{0,1:T(8,128)(2,1)} async-done(((bf16[256,128]{0,1:T(8,128)(2,1)}), bf16[16384,128]{0,1:T(8,128)(2,1)}) %all-gather.6.cloned.1.call-update) | async-done | bytes 4194320 | tf_op jit(solution)/shard_map/all_gather | solution.py:72
  425.2 3.3 convolution_subtract_fusion.1
  428.6 2.0 copy-done.2
  431.5 11.7 %cholesky.55 = f32[128,128]{1,0:T(8,128)S(1)} custom-call(f32[128,128]{1,0:T(8,128)S(1)} %fusion.12), custom_call_target="Cholesky" | custom-call | tf_op jit(solution)/shard_map/jit(cholesky)/cholesky | solution.py:59
  443.9 1.3 select_select_fusion
  445.3 170.2 %all-reduce.10.cloned.1.call-done = f32[128,128]{1,0:T(8,128)} async-done(((f32[128,128]{1,0:T(8,128)}), f32[128,128]{1,0:T(8,128)}) %all-reduce.10.cloned.1.call-update) | async-done | bytes 65552 | tf_op jit(solution)/shard_map/psum | solution.py:11
  616.3 9.8 %custom-call.7 = f32[1,128,128]{1,2,0:T(8,128)S(1)} custom-call(f32[1,128,128]{2,1,0:T(8,128)S(1)} %select_bitcast_fusion), custom_call_target="InvertDiagBlocksLowerTriangular" | custom-call | tf_op jit(solution)/shard_map/jit(_solve_triangular)/triangular_solve | solution.py:61
  627.3 1.9 convert_select_fusion
  629.2 41.2 %all-reduce.12.cloned.1.call-done = bf16[256,128]{0,1:T(8,128)(2,1)} async-done(((bf16[256,128]{0,1:T(8,128)(2,1)}), bf16[256,128]{0,1:T(8,128)(2,1)}) %all-reduce.12.cloned.1.call-update) | async-done | bytes 65552 | tf_op jit(solution)/shard_map/psum | solution.py:11
  670.4 81.4 %all-gather.8.cloned.1.call-done = bf16[16384,128]{0,1:T(8,128)(2,1)} async-done(((bf16[256,128]{0,1:T(8,128)(2,1)}), bf16[16384,128]{0,1:T(8,128)(2,1)}) %all-gather.8.cloned.1.call-update) | async-done | bytes 4194320 | tf_op jit(solution)/shard_map/all_gather | solution.py:72
  751.8 4.6 fusion.1
  756.3 5.6 copy.18
  (47 shorter events, 11.2 us)
Async XLA Ops:
  6.5 17.5 %copy-start = (f32[16384]{0:T(1024)S(1)}, f32[16384]{0:T(1024)}, u32[]{:S(2)}) copy-start(f32[16384]{0:T(1024)} %param.11) | copy-start | bytes 196612
  6.5 17.5 %copy-start.3 = (s32[128]{0:T(128)S(1)}, s32[128]{0:T(128)}, u32[]{:S(2)}) copy-start(s32[128]{0:T(128)} %param.12) | copy-start | bytes 1540
  6.5 91.6 %all-gather.4.cloned.1.call-start = ((), (), s32[]{:S(2)}) async-start(), calls=%async_computation.1 | async-start | bytes 8519680 | tf_op jit(solution)/shard_map/all_gather | solution.py:44
  10.9 32.7 %all-to-all-start = ((bf16[16,64,256]{2,0,1:T(8,128)(2,1)}), bf16[16,64,256]{2,0,1:T(8,128)(2,1)S(1)}, u32[]{:S(2)}, u32[]{:S(2)}) async-start(bf16[16,64,256]{2,0,1:T(8,128)(2,1)} %copy.12), calls=%async_computation | async-start | bytes 1048576 | tf_op jit(solution)/shard_map/all_to_all | solution.py:42
  23.9 265.1 %all-reduce.6.cloned.1.call-start = ((), (), s32[]{:S(2)}) async-start(), calls=%async_computation.2 | async-start | bytes 131072 | tf_op jit(solution)/shard_map/psum | solution.py:11
  104.8 2.0 copy-start.1
  121.5 222.5 %all-reduce.8.cloned.1.call-start = ((), (), s32[]{:S(2)}) async-start(), calls=%async_computation.3 | async-start | bytes 131072 | tf_op jit(solution)/shard_map/psum | solution.py:11
  302.8 122.5 %all-gather.6.cloned.1.call-start = ((), (), s32[]{:S(2)}) async-start(), calls=%async_computation.4 | async-start | bytes 4259840 | tf_op jit(solution)/shard_map/all_gather | solution.py:72
  344.0 271.4 %all-reduce.10.cloned.1.call-start = ((), (), s32[]{:S(2)}) async-start(), calls=%async_computation.5 | async-start | bytes 131072 | tf_op jit(solution)/shard_map/psum | solution.py:11
  428.5 2.0 copy-start.2
  445.2 225.1 %all-reduce.12.cloned.1.call-start = ((), (), s32[]{:S(2)}) async-start(), calls=%async_computation.6 | async-start | bytes 131072 | tf_op jit(solution)/shard_map/psum | solution.py:11
  629.1 122.6 %all-gather.8.cloned.1.call-start = ((), (), s32[]{:S(2)}) async-start(), calls=%async_computation.7 | async-start | bytes 4259840 | tf_op jit(solution)/shard_map/all_gather | solution.py:72
Sparse Core Ops, SparseCore 0:
  10.1 88.0 all-gather.3
  121.6 167.4 all-reduce.5
  302.9 41.0 all-reduce.7
  346.4 78.8 all-gather.5
  445.3 170.0 all-reduce.9
  629.3 41.0 all-reduce.11
  672.9 78.8 all-gather.7
where the time goes:
time: 769 us
  waiting for transfers between devices  656 us (85%)
  other arithmetic  51.1 us (7%)
  matrix products  22.1 us (3%)
  between operations  13.7 us (2%)
  starting transfers between devices  13.4 us (2%)
  local copies, waits for them, and re-layouts  12.1 us (2%)
    psum x4, waiting for transfers between devices, spread(): return lax.psum(kept, axis)  420 us
    all_gather x2, waiting for transfers between devices, local(): everyone = lax.all_gather(across, 'link', axis=0, tiled=True)  162 us
    all_gather x1, waiting for transfers between devices, local(): lax.all_gather(col_slab, 'link', axis=0, tiled=True)  54.6 us
    another operation x6, other arithmetic, local(): factor_local = jnp.linalg.cholesky(diag_block)  24.8 us
    another operation x4, other arithmetic, local(): jax.scipy.linalg.solve_triangular(lower_fac, matrix[:, first_col:first_co...  21.3 us
    all_to_all x1, waiting for transfers between devices, local(): lax.all_to_all(own_dense, 'link', split_axis=1, concat_axis=0, tiled=True)  19.3 us
  transfers between devices with their start and end apart: 8, of which 8 were waited for; matrix products, arithmetic and copies ran while one was open for 0% of the time, Pallas kernels for 0%

commit v1 on v0

--- a/solution.py
+++ b/solution.py
@@ -2,13 +2,18 @@
 import jax.numpy as jnp
 from jax import lax
 from jax.sharding import PartitionSpec as P
+from jax.lax import all_gather
 
 PANEL = 128
 
 
+def wait_the_pools(buf, row_axis):
+    return all_gather(buf, row_axis).sum(axis=0)
+
+
 def spread(value, axis, source):
     kept = jnp.where(lax.axis_index(axis) == source, value, 0).astype(value.dtype)
-    return lax.psum(kept, axis)
+    return wait_the_pools(kept, axis)
 
 
 def densify(tile_vals, tile_ids, targets):

time: 769 us -> 514 us (0.67)
  waiting for transfers between devices: 656 us -> 379 us
  blocking collectives: 0 us -> 20.7 us
    psum x4 -> x0, waiting for transfers between devices: 420 us -> none  [spread(): return lax.psum(kept, axis)]
    all_gather x0 -> x2, waiting for transfers between devices: none -> 154 us  [wait_the_pools(): return all_gather(buf, row_axis).sum(axis=0)]
    all_gather x0 -> x2, blocking collectives: none -> 20.7 us  [wait_the_pools(): return all_gather(buf, row_axis).sum(axis=0)]
    all_gather x2, waiting for transfers between devices: 162 us -> 150 us  [local(): everyone = lax.all_gather(across, 'link', axis=0, tiled=True)]
  transfers between devices with their start and end apart: 8 -> 6, of which waited for: 8 -> 6; matrix products, arithmetic and copies ran while one was open for 0% -> 0% of each run, Pallas kernels for 0% -> 0%
where the time goes in v1:
time: 514 us
  waiting for transfers between devices  379 us (74%)
  other arithmetic  56 us (11%)
  blocking collectives  20.7 us (4%)
  matrix products  19.1 us (4%)
  between operations  13.4 us (3%)
  starting transfers between devices  13.3 us (3%)
  local copies, waits for them, and re-layouts  12.5 us (2%)
    all_gather x2, waiting for transfers between devices, wait_the_pools(): return all_gather(buf, row_axis).sum(axis=0)  154 us
    all_gather x2, waiting for transfers between devices, local(): everyone = lax.all_gather(across, 'link', axis=0, tiled=True)  150 us
    all_gather x1, waiting for transfers between devices, local(): lax.all_gather(col_slab, 'link', axis=0, tiled=True)  54.5 us
    another operation x6, other arithmetic, local(): factor_local = jnp.linalg.cholesky(diag_block)  24.8 us
    all_gather x2, blocking collectives, wait_the_pools(): return all_gather(buf, row_axis).sum(axis=0)  20.7 us
    another operation x4, other arithmetic, local(): jax.scipy.linalg.solve_triangular(lower_fac, matrix[:, first_col:first_co...  19.6 us
    all_to_all x1, waiting for transfers between devices, local(): lax.all_to_all(own_dense, 'link', split_axis=1, concat_axis=0, tiled=True)  19.3 us
    all_to_all x1, starting transfers between devices, local(): lax.all_to_all(own_dense, 'link', split_axis=1, concat_axis=0, tiled=True)  13 us
  transfers between devices with their start and end apart: 6, of which 6 were waited for; matrix products, arithmetic and copies ran while one was open for 0% of the time, Pallas kernels for 0%

profile of v1, /device:TPU:1, one launch (start us, length us, event | category | flops | bytes accessed | tf_op | source)
XLA Modules:
  0.0 513.7 jit_solution(5185980086118882535)
XLA Ops:
  7.2 1.4 convolution_convert_fusion
  11.0 13.0 %all-to-all-start = ((bf16[16,64,256]{2,0,1:T(8,128)(2,1)}), bf16[16,64,256]{2,0,1:T(8,128)(2,1)S(1)}, u32[]{:S(2)}, u32[]{:S(2)}) async-start(bf16[16,64,256]{2,0,1:T(8,128)(2,1)} %copy.19), calls=%async_computation | async-start | bytes 1048576 | tf_op jit(solution)/shard_map/all_to_all | solution.py:47
  24.4 19.3 %all-to-all-done = bf16[16,64,256]{2,0,1:T(8,128)(2,1)S(1)} async-done(((bf16[16,64,256]{2,0,1:T(8,128)(2,1)}), bf16[16,64,256]{2,0,1:T(8,128)(2,1)S(1)}, u32[]{:S(2)}, u32[]{:S(2)}) %all-to-all-start) | async-done | bytes 524320 | tf_op jit(solution)/shard_map/all_to_all | solution.py:47
  43.6 54.5 %all-gather.10.cloned.1.call-done = bf16[1024,4096]{1,0:T(8,128)(2,1)} async-done(((bf16[16,4096]{1,0:T(8,128)(2,1)}), bf16[1024,4096]{1,0:T(8,128)(2,1)}) %all-gather.10.cloned.1.call-update) | async-done | bytes 8388624 | tf_op jit(solution)/shard_map/all_gather | solution.py:49
  98.2 6.6 %convolution_add_fusion = f32[256,4096]{0,1:T(8,128)S(1)} fusion(bf16[1024,256]{1,0:T(8,128)(2,1)S(1)} %bitcast.72, bf16[1024,4096]{1,0:T(8,128)(2,1)} %all-gather.10.cloned.1.call-done, f32[256]{0:T(256)S(1)} %dynamic_slice.13, s32[256]{0:T(256)S(1)} %iota_add_fusion.1, s32[4096]{0:T(1024)S(1)} %iota_add_fusion), kind=kOutput, calls=%fused_computation.4 | convolution fusion | flops 2150629376 | bytes 13125632 | tf_op jit(solution)/shard_map/dot_general | solution.py:27
  104.8 2.0 copy-done.2
  107.8 11.7 %cholesky.44 = f32[128,128]{1,0:T(8,128)S(1)} custom-call(f32[128,128]{1,0:T(8,128)S(1)} %fusion.14), custom_call_target="Cholesky" | custom-call | tf_op jit(solution)/shard_map/jit(cholesky)/cholesky | solution.py:64
  121.5 75.9 %all-gather.16.cloned.1.call-done = f32[8192,128]{1,0:T(8,128)} async-done(((f32[128,128]{1,0:T(8,128)}), f32[8192,128]{1,0:T(8,128)}) %all-gather.16.cloned.1.call-update) | async-done | bytes 4194320 | tf_op jit(solution)/shard_map/all_gather | solution.py:11
  197.3 2.4 reduce_sum.42
  200.1 9.8 %custom-call.6 = f32[1,128,128]{1,2,0:T(8,128)S(1)} custom-call(f32[1,128,128]{2,1,0:T(8,128)S(1)} %select_bitcast_fusion.1), custom_call_target="InvertDiagBlocksLowerTriangular" | custom-call | tf_op jit(solution)/shard_map/jit(_solve_triangular)/triangular_solve | solution.py:66
  209.9 1.2 convert_select_fusion.1
  211.1 10.3 %all-gather.1 = bf16[1024,128]{0,1:T(8,128)(2,1)S(1)} all-gather(bf16[256,128]{0,1:T(8,128)(2,1)S(1)} %get-tuple-element.6), channel_id=3, replica_groups=mesh['link'=64,'col'=4] {'col'}, dimensions={0}, use_global_device_ids=true | all-gather | bytes 327680 | tf_op jit(solution)/shard_map/all_gather | solution.py:11
  222.8 75.1 %all-gather.12.cloned.1.call-done = bf16[16384,128]{0,1:T(8,128)(2,1)} async-done(((bf16[256,128]{0,1:T(8,128)(2,1)}), bf16[16384,128]{0,1:T(8,128)(2,1)}) %all-gather.12.cloned.1.call-update) | async-done | bytes 4194320 | tf_op jit(solution)/shard_map/all_gather | solution.py:77
  297.9 3.3 convolution_subtract_fusion.1
  301.2 2.0 copy-done.1
  304.2 11.7 %cholesky.55 = f32[128,128]{1,0:T(8,128)S(1)} custom-call(f32[128,128]{1,0:T(8,128)S(1)} %fusion.12), custom_call_target="Cholesky" | custom-call | tf_op jit(solution)/shard_map/jit(cholesky)/cholesky | solution.py:64
  317.9 78.5 %all-gather.18.cloned.1.call-done = f32[8192,128]{1,0:T(8,128)} async-done(((f32[128,128]{1,0:T(8,128)}), f32[8192,128]{1,0:T(8,128)}) %all-gather.18.cloned.1.call-update) | async-done | bytes 4194320 | tf_op jit(solution)/shard_map/all_gather | solution.py:11
  396.4 2.4 reduce_sum.44
  399.2 9.8 %custom-call.7 = f32[1,128,128]{1,2,0:T(8,128)S(1)} custom-call(f32[1,128,128]{2,1,0:T(8,128)S(1)} %select_bitcast_fusion), custom_call_target="InvertDiagBlocksLowerTriangular" | custom-call | tf_op jit(solution)/shard_map/jit(_solve_triangular)/triangular_solve | solution.py:66
  409.0 1.2 convert_select_fusion
  410.2 10.3 %all-gather.3 = bf16[1024,128]{0,1:T(8,128)(2,1)S(1)} all-gather(bf16[256,128]{0,1:T(8,128)(2,1)S(1)} %get-tuple-element.9), channel_id=5, replica_groups=mesh['link'=64,'col'=4] {'col'}, dimensions={0}, use_global_device_ids=true | all-gather | bytes 327680 | tf_op jit(solution)/shard_map/all_gather | solution.py:11
  421.7 75.3 %all-gather.14.cloned.1.call-done = bf16[16384,128]{0,1:T(8,128)(2,1)} async-done(((bf16[256,128]{0,1:T(8,128)(2,1)}), bf16[16384,128]{0,1:T(8,128)(2,1)}) %all-gather.14.cloned.1.call-update) | async-done | bytes 4194320 | tf_op jit(solution)/shard_map/all_gather | solution.py:77
  497.0 4.5 fusion.1
  501.6 5.6 %copy.25 = f32[256,4096]{1,0:T(8,128)} copy(f32[256,4096]{0,1:T(8,128)} %fusion.1) | data formatting | bytes 8388608 | tf_op jit(solution)/shard_map/jit(_where)/select_n | solution.py:85
  (49 shorter events, 12.3 us)
Async XLA Ops:
  6.5 17.5 %copy-start = (f32[16384]{0:T(1024)S(1)}, f32[16384]{0:T(1024)}, u32[]{:S(2)}) copy-start(f32[16384]{0:T(1024)} %param.11) | copy-start | bytes 196612
  6.5 17.5 %copy-start.3 = (s32[128]{0:T(128)S(1)}, s32[128]{0:T(128)}, u32[]{:S(2)}) copy-start(s32[128]{0:T(128)} %param.12) | copy-start | bytes 1540
  6.5 91.6 %all-gather.10.cloned.1.call-start = ((), (), s32[]{:S(2)}) async-start(), calls=%async_computation.1 | async-start | bytes 8519680 | tf_op jit(solution)/shard_map/all_gather | solution.py:49
  11.0 32.7 %all-to-all-start = ((bf16[16,64,256]{2,0,1:T(8,128)(2,1)}), bf16[16,64,256]{2,0,1:T(8,128)(2,1)S(1)}, u32[]{:S(2)}, u32[]{:S(2)}) async-start(bf16[16,64,256]{2,0,1:T(8,128)(2,1)} %copy.19), calls=%async_computation | async-start | bytes 1048576 | tf_op jit(solution)/shard_map/all_to_all | solution.py:47
  23.9 173.4 %all-gather.16.cloned.1.call-start = ((), (), s32[]{:S(2)}) async-start(), calls=%async_computation.4 | async-start | bytes 4259840 | tf_op jit(solution)/shard_map/all_gather | solution.py:11
  104.8 2.0 copy-start.2
  121.4 176.5 %all-gather.12.cloned.1.call-start = ((), (), s32[]{:S(2)}) async-start(), calls=%async_computation.2 | async-start | bytes 4259840 | tf_op jit(solution)/shard_map/all_gather | solution.py:77
  222.6 173.8 %all-gather.18.cloned.1.call-start = ((), (), s32[]{:S(2)}) async-start(), calls=%async_computation.5 | async-start | bytes 4259840 | tf_op jit(solution)/shard_map/all_gather | solution.py:11
  301.2 2.0 copy-start.1
  317.8 179.2 %all-gather.14.cloned.1.call-start = ((), (), s32[]{:S(2)}) async-start(), calls=%async_computation.3 | async-start | bytes 4259840 | tf_op jit(solution)/shard_map/all_gather | solution.py:77
Sparse Core Ops, SparseCore 0:
  10.1 88.0 all-gather.9
  121.5 75.7 all-gather.15
  222.7 75.1 all-gather.11
  317.9 78.4 all-gather.17
  421.8 75.1 all-gather.13
